TPU v7x, 512 devices: a whole 4x4x16 slice. The times are simulated.
512 devices in a mesh: leaf: 32 (over z, core), sub: 16 (over x, y).
Axes of the slice: x: 4, y: 4, z: 16, core: 2. Of those that a mesh axis runs over, the one named last changes fastest.
Arguments:
- right_side: float32 [2048, 32, 256], P(('leaf', 'sub'))
- points: float32 [2048, 3, 256], P(('leaf', 'sub')), may hold values from 0 to 32, as said below
- near_boxes: int32 [2048, 27], P(('leaf', 'sub')), may hold values from -1 to 2047, as said below
Outputs:
- solution_field: float32 [2048, 32, 256], P(('leaf', 'sub'))
- residual: float32 [2048, 32, 256], P(('leaf', 'sub'))
Inputs may be any that keep to these rules, and one draw needn't show every extreme that they name: `near_boxes`: each box's points lie in one unit cube with integer corner. A box lists itself and exactly the boxes whose cubes touch its own (faces, edges or corners), and -1 in its other entries. Every listed box lies on a device whose grid position differs by at most one in each of the three grid dimensions, where a device's index over leaf+sub is gx * 4 * 8 + gy * 8 + gz. Each box's points lie in its unit cube, the cubes of one device forming a block of 2 x 2 x 1.
All inputs are finite; a program needn't handle non-finite values.
Results may differ from a plain program's by a relative error of at most 0.0003.
Values sent between devices are 32-bit elements; how exact they have to be, the bound alone decides.
No kernel may reach another device: no remote copies, remote signals or barrier semaphores. Data moves between devices by JAX's collectives and lax.ppermute only.
A program may use at most 64 MiB of HBM per device.

v0:
```python
import jax
import jax.numpy as jnp
from jax import lax
from jax.sharding import PartitionSpec as P

ITERS = 2
GRID_Y = 4
NOISE_LEVEL = 0.3
KERNEL_SCALE = 0.15
SUPPORT = 0.5


def passed_along(block, axis, distance):
    devices = range(lax.axis_size(axis))
    route = [(i - distance, i) for i in devices if i - distance in devices]
    return lax.ppermute(block, axis, route)


def wendland(centers, others):
    summed = jnp.zeros((others.shape[0], others.shape[2], centers.shape[1]), jnp.float32)
    for component in range(3):
        difference = others[:, component, :, None] - centers[component][None, None, :]
        summed = summed + difference * difference
    radius = jnp.sqrt(summed) / SUPPORT
    inside = jnp.maximum(1.0 - radius, 0.0)
    return inside * inside * inside * inside * (4.0 * radius + 1.0)


def apply_box(entry):
    centers, others, near_values = entry
    kernel = wendland(centers, others)
    return jnp.einsum(
        "mrj,mji->ri",
        near_values,
        kernel,
        precision=lax.Precision.HIGHEST,
        preferred_element_type=jnp.float32,
    )


def grid_offsets(count_mid, count_low):
    listing = []
    for step_x in (-1, 0, 1):
        for step_y in (-1, 0, 1):
            for step_z in (-1, 0, 1):
                listing.append(step_x * count_mid * count_low + step_y * count_low + step_z)
    return listing


def collect_direct(tile_in, count_mid, count_low, mover):
    pieces = []
    for offset in grid_offsets(count_mid, count_low):
        if offset == 0:
            pieces.append(tile_in)
        else:
            pieces.append(mover(tile_in, -offset))
    stacked = jnp.stack(pieces, axis=0)
    return stacked.reshape((-1,) + tile_in.shape[1:])


def locate(near_boxes, per_dev, count_mid, count_low):
    own_dev = lax.axis_index(("leaf", "sub"))
    present = (near_boxes >= 0).astype(jnp.float32)
    clamped = jnp.maximum(near_boxes, 0)
    owner_dev = clamped // per_dev
    plane = count_mid * count_low
    step_x = owner_dev // plane - own_dev // plane
    step_y = owner_dev // count_low % count_mid - own_dev // count_low % count_mid
    step_z = owner_dev % count_low - own_dev % count_low
    positions = (((step_x + 1) * 3 + step_y + 1) * 3 + step_z + 1) * per_dev + clamped % per_dev
    positions = jnp.clip(positions, 0, 27 * per_dev - 1)
    return (positions, present)


def column_sums(first, second):
    return jnp.sum(first * second, axis=(0, 2))


def spread(column):
    return column[None, :, None]


def squares(residual):
    return lax.psum(column_sums(residual, residual), ("leaf", "sub"))


def per_device(right_side, points, near_boxes):
    count_low = lax.axis_size("sub") // 2
    count_mid = GRID_Y
    per_dev = points.shape[0]
    point_tiles = collect_direct(
        points,
        count_mid,
        count_low,
        lambda moving, amount: passed_along(moving, ("leaf", "sub"), amount),
    )
    positions, present = locate(near_boxes, per_dev, count_mid, count_low)
    others = point_tiles[positions]
    solution_field = jnp.zeros_like(right_side)
    residual = right_side
    direction = right_side
    norm_now = squares(residual)
    for iteration in range(ITERS):
        gathered = collect_direct(
            direction,
            count_mid,
            count_low,
            lambda moving, amount: passed_along(moving, ("leaf", "sub"), amount),
        )
        near_values = gathered[positions] * present[:, :, None, None]
        products = lax.map(apply_box, (points, others, near_values))
        image_vec = KERNEL_SCALE * products + NOISE_LEVEL * direction
        curve = lax.psum(column_sums(direction, image_vec), ("leaf", "sub"))
        step_size = norm_now / curve
        solution_field = solution_field + spread(step_size) * direction
        residual = residual - spread(step_size) * image_vec
        norm_next = squares(residual)
        direction = residual + spread(norm_next / norm_now) * direction
        norm_now = norm_next
    return (solution_field, residual)


def solution(mesh):
    placed = (
        P(("leaf", "sub"), None, None),
        P(("leaf", "sub"), None, None),
        P(("leaf", "sub"), None),
    )
    return jax.shard_map(
        per_device,
        mesh=mesh,
        in_specs=placed,
        out_specs=(P(("leaf", "sub"), None, None), P(("leaf", "sub"), None, None)),
        check_vma=False,
    )
```

profile of v0, /device:TPU:1, one launch (start us, length us, event | category | flops | bytes accessed | tf_op | source)
XLA Modules:
  0.0 891.9 jit_solution(12877085652996151127)
XLA Ops:
  0.6 8.0 collective-permute-start
  8.6 5.4 collective-permute-start.1
  14.0 6.2 collective-permute-start.2
  20.2 5.7 collective-permute-start.3
  26.0 4.2 collective-permute-start.26
  32.3 6.3 collective-permute-start.27
  39.7 6.2 collective-permute-start.28
  46.9 8.3 collective-permute-start.29
  56.2 7.1 collective-permute-start.30
  64.4 6.0 collective-permute-start.31
  71.4 7.3 collective-permute-start.32
  79.7 11.5 %collective-permute-start.33 = (f32[4,3,256]{2,0,1:T(4,128)}, f32[4,3,256]{2,0,1:T(4,128)S(1)}, u32[]{:S(2)}, u32[]{:S(2)}) collective-permute-start(f32[4,3,256]{2,0,1:T(4,128)} %param.8), channel_id=1, source_target_pairs={{0,24},{1,25},{2,26},{3,27},{4,28},{5,29},{6,30},{7,31},{8,32},{9,... | collective-permute-start | bytes 36872 | tf_op jit(solution)/shard_map/ppermute | solution.py:16
  92.2 4.4 collective-permute-start.34
  97.6 6.2 collective-permute-start.35
  105.0 6.2 collective-permute-start.36
  112.2 5.7 collective-permute-start.37
  120.4 4.5 collective-permute-start.38
  124.9 4.0 collective-permute-done.38
  128.9 3.6 collective-permute-start.39
  133.6 5.0 collective-permute-start.40
  140.6 5.9 collective-permute-start.41
  146.5 5.9 collective-permute-done.41
  154.4 6.2 collective-permute-done.42
  161.8 7.6 collective-permute-done.43
  170.7 9.7 %collective-permute-done.44 = f32[4,3,256]{2,0,1:T(4,128)S(1)} collective-permute-done((f32[4,3,256]{2,0,1:T(4,128)}, f32[4,3,256]{2,0,1:T(4,128)S(1)}, u32[]{:S(2)}, u32[]{:S(2)}) %collective-permute-start.44) | collective-permute-done | bytes 12320 | tf_op jit(solution)/shard_map/ppermute | solution.py:16
  181.7 7.2 collective-permute-done.45
  190.2 18.6 %collective-permute-done.46 = f32[4,3,256]{2,0,1:T(4,128)S(1)} collective-permute-done((f32[4,3,256]{2,0,1:T(4,128)}, f32[4,3,256]{2,0,1:T(4,128)S(1)}, u32[]{:S(2)}, u32[]{:S(2)}) %collective-permute-start.46) | collective-permute-done | bytes 12320 | tf_op jit(solution)/shard_map/ppermute | solution.py:16
  210.1 10.7 %collective-permute-done.47 = f32[4,3,256]{2,0,1:T(4,128)S(1)} collective-permute-done((f32[4,3,256]{2,0,1:T(4,128)}, f32[4,3,256]{2,0,1:T(4,128)S(1)}, u32[]{:S(2)}, u32[]{:S(2)}) %collective-permute-start.47) | collective-permute-done | bytes 12320 | tf_op jit(solution)/shard_map/ppermute | solution.py:16
  222.1 4.2 collective-permute-done.48
  227.7 7.8 collective-permute-done.49
  236.8 11.9 %collective-permute-done.50 = f32[4,3,256]{2,0,1:T(4,128)S(1)} collective-permute-done((f32[4,3,256]{2,0,1:T(4,128)}, f32[4,3,256]{2,0,1:T(4,128)S(1)}, u32[]{:S(2)}, u32[]{:S(2)}) %collective-permute-start.50) | collective-permute-done | bytes 12320 | tf_op jit(solution)/shard_map/ppermute | solution.py:16
  250.0 7.1 collective-permute-done.51
  257.0 4.1 collective-permute-start.4
  263.0 6.4 collective-permute-start.5
  269.4 11.4 %collective-permute-start.6 = (f32[4,32,256]{2,1,0:T(8,128)S(1)}, f32[4,32,256]{2,1,0:T(8,128)S(1)}, u32[]{:S(2)}, u32[]{:S(2)}) collective-permute-start(f32[4,32,256]{2,1,0:T(8,128)S(1)} %copy-done.2), channel_id=1, source_target_pairs={{0,25},{1,26},{2,27},{3,28},{4,29},{5,30},{6,31},{7,32},{8,33},{9,... | collective-permute-start | bytes 393224 | tf_op jit(solution)/shard_map/ppermute | solution.py:16
  282.8 7.2 collective-permute-start.8
  292.1 5.5 collective-permute-start.10
  302.7 5.8 collective-permute-start.13
  311.5 4.0 collective-permute-start.15
  337.4 5.4 collective-permute-done.21
  343.5 4.2 collective-permute-done.24
  355.1 43.8 %while.24 = (s32[]{:T(128)}, f32[4,32,256]{2,1,0:T(8,128)S(1)}, f32[4,27,32,256]{3,2,1,0:T(8,128)}, f32[4,27,3,256]{3,1,2,0:T(8,128)}, f32[4,3,256]{2,0,1:T(4,128)S(1)}, /*index=5*/s32[]{:T(128)}, s32[]{:T(128)}, s32[]{}, s32[]{}) while((s32[]{:T(128)}, f32[4,32,256]{2,1,0:T(8,128)S(1)}, f32[4,27,32,256]{3,2,1,0:T(8,128)}, ...), condition=%wide.region_3.4_spmd, body=%wide.region_2.3_spmd.sunk | while | flops 709558272 | bytes 1357957 | solution.py:111
  356.1 10.0 %fusion.104 = f32[4,32,256]{2,1,0:T(8,128)S(1)} fusion(f32[4,32,256]{2,1,0:T(8,128)S(1)} %get-tuple-element.288, s32[]{:T(128)} %get-tuple-element.287, f32[256]{0:T(256)S(1)} %bitcast.242, f32[27,256]{1,0:T(8,128)S(1)} %get-tuple-element.262, f32[256]{0:T(256)S(1)} %bitcast.241, f32[27,256]{1,0:T(8,128)S(1)} %get-tuple-element.264, ...), kind=kOutput, calls=%fused_computation.31.clone.1 | convolution fusion | flops 709558272 | bytes 1019904 | tf_op jit(solution)/shard_map/while/body/eval_jaxpr/mrj,mji->ri/dot_general | solution.py:32
  367.0 10.0 %fusion.104 = f32[4,32,256]{2,1,0:T(8,128)S(1)} fusion(f32[4,32,256]{2,1,0:T(8,128)S(1)} %get-tuple-element.288, s32[]{:T(128)} %get-tuple-element.287, f32[256]{0:T(256)S(1)} %bitcast.242, f32[27,256]{1,0:T(8,128)S(1)} %get-tuple-element.262, f32[256]{0:T(256)S(1)} %bitcast.241, f32[27,256]{1,0:T(8,128)S(1)} %get-tuple-element.264, ...), kind=kOutput, calls=%fused_computation.31.clone.1 | convolution fusion | flops 709558272 | bytes 1019904 | tf_op jit(solution)/shard_map/while/body/eval_jaxpr/mrj,mji->ri/dot_general | solution.py:32
  378.0 10.0 %fusion.104 = f32[4,32,256]{2,1,0:T(8,128)S(1)} fusion(f32[4,32,256]{2,1,0:T(8,128)S(1)} %get-tuple-element.288, s32[]{:T(128)} %get-tuple-element.287, f32[256]{0:T(256)S(1)} %bitcast.242, f32[27,256]{1,0:T(8,128)S(1)} %get-tuple-element.262, f32[256]{0:T(256)S(1)} %bitcast.241, f32[27,256]{1,0:T(8,128)S(1)} %get-tuple-element.264, ...), kind=kOutput, calls=%fused_computation.31.clone.1 | convolution fusion | flops 709558272 | bytes 1019904 | tf_op jit(solution)/shard_map/while/body/eval_jaxpr/mrj,mji->ri/dot_general | solution.py:32
  388.9 10.0 %fusion.104 = f32[4,32,256]{2,1,0:T(8,128)S(1)} fusion(f32[4,32,256]{2,1,0:T(8,128)S(1)} %get-tuple-element.288, s32[]{:T(128)} %get-tuple-element.287, f32[256]{0:T(256)S(1)} %bitcast.242, f32[27,256]{1,0:T(8,128)S(1)} %get-tuple-element.262, f32[256]{0:T(256)S(1)} %bitcast.241, f32[27,256]{1,0:T(8,128)S(1)} %get-tuple-element.264, ...), kind=kOutput, calls=%fused_computation.31.clone.1 | convolution fusion | flops 709558272 | bytes 1019904 | tf_op jit(solution)/shard_map/while/body/eval_jaxpr/mrj,mji->ri/dot_general | solution.py:32
  399.1 121.1 %all-reduce = (f32[32]{0:T(128)S(1)}, f32[32]{0:T(128)S(1)}) all-reduce(f32[32]{0:T(128)S(1)} %get-tuple-element.155, f32[32]{0:T(128)S(1)} %get-tuple-element.154), channel_id=1, replica_groups=mesh['leaf'=32,'sub'=16] {'leaf','sub'}, use_global_device_ids=true, to_apply=%region_1.2 | all-reduce | flops 64 | bytes 512 | tf_op jit(solution)/shard_map/psum | solution.py:84
  520.4 99.5 %psum.30 = f32[32]{0:T(128)S(1)} all-reduce(f32[32]{0:T(128)S(1)} %multiply_reduce_fusion.1), channel_id=1, replica_groups=mesh['leaf'=32,'sub'=16] {'leaf','sub'}, use_global_device_ids=true, to_apply=%region_7.8 | all-reduce | flops 32 | bytes 256 | tf_op jit(solution)/shard_map/psum | solution.py:84
  620.6 5.1 collective-permute-start.52
  625.6 3.6 collective-permute-start.53
  632.6 5.3 collective-permute-start.55
  640.4 7.1 collective-permute-start.57
  650.4 4.3 collective-permute-start.59
  654.7 5.2 collective-permute-start.60
  659.9 4.2 collective-permute-start.61
  667.3 4.0 collective-permute-start.63
  673.4 7.0 collective-permute-start.65
  682.3 4.4 collective-permute-start.67
  728.6 43.9 %while.25 = (s32[]{:T(128)}, f32[4,32,256]{2,1,0:T(8,128)S(1)}, f32[4,27,32,256]{3,2,1,0:T(8,128)}, f32[4,27,3,256]{3,1,2,0:T(8,128)}, f32[4,3,256]{2,0,1:T(4,128)S(1)}, /*index=5*/s32[]{:T(128)}, s32[]{:T(128)}, s32[]{}, s32[]{}) while((s32[]{:T(128)}, f32[4,32,256]{2,1,0:T(8,128)S(1)}, f32[4,27,32,256]{3,2,1,0:T(8,128)}, ...), condition=%wide.region_9.10_spmd, body=%wide.region_8.9_spmd.sunk | while | flops 709558272 | bytes 1357957 | solution.py:111
  729.7 10.0 %fusion.107 = f32[4,32,256]{2,1,0:T(8,128)S(1)} fusion(f32[4,32,256]{2,1,0:T(8,128)S(1)} %get-tuple-element.315, s32[]{:T(128)} %get-tuple-element.314, f32[256]{0:T(256)S(1)} %bitcast.245, f32[27,256]{1,0:T(8,128)S(1)} %get-tuple-element.273, f32[256]{0:T(256)S(1)} %bitcast.244, f32[27,256]{1,0:T(8,128)S(1)} %get-tuple-element.275, ...), kind=kOutput, calls=%fused_computation.74.clone.1 | convolution fusion | flops 709558272 | bytes 1019904 | tf_op jit(solution)/shard_map/while/body/eval_jaxpr/mrj,mji->ri/dot_general | solution.py:32
  740.6 10.0 %fusion.107 = f32[4,32,256]{2,1,0:T(8,128)S(1)} fusion(f32[4,32,256]{2,1,0:T(8,128)S(1)} %get-tuple-element.315, s32[]{:T(128)} %get-tuple-element.314, f32[256]{0:T(256)S(1)} %bitcast.245, f32[27,256]{1,0:T(8,128)S(1)} %get-tuple-element.273, f32[256]{0:T(256)S(1)} %bitcast.244, f32[27,256]{1,0:T(8,128)S(1)} %get-tuple-element.275, ...), kind=kOutput, calls=%fused_computation.74.clone.1 | convolution fusion | flops 709558272 | bytes 1019904 | tf_op jit(solution)/shard_map/while/body/eval_jaxpr/mrj,mji->ri/dot_general | solution.py:32
  751.6 10.0 %fusion.107 = f32[4,32,256]{2,1,0:T(8,128)S(1)} fusion(f32[4,32,256]{2,1,0:T(8,128)S(1)} %get-tuple-element.315, s32[]{:T(128)} %get-tuple-element.314, f32[256]{0:T(256)S(1)} %bitcast.245, f32[27,256]{1,0:T(8,128)S(1)} %get-tuple-element.273, f32[256]{0:T(256)S(1)} %bitcast.244, f32[27,256]{1,0:T(8,128)S(1)} %get-tuple-element.275, ...), kind=kOutput, calls=%fused_computation.74.clone.1 | convolution fusion | flops 709558272 | bytes 1019904 | tf_op jit(solution)/shard_map/while/body/eval_jaxpr/mrj,mji->ri/dot_general | solution.py:32
  762.5 10.0 %fusion.107 = f32[4,32,256]{2,1,0:T(8,128)S(1)} fusion(f32[4,32,256]{2,1,0:T(8,128)S(1)} %get-tuple-element.315, s32[]{:T(128)} %get-tuple-element.314, f32[256]{0:T(256)S(1)} %bitcast.245, f32[27,256]{1,0:T(8,128)S(1)} %get-tuple-element.273, f32[256]{0:T(256)S(1)} %bitcast.244, f32[27,256]{1,0:T(8,128)S(1)} %get-tuple-element.275, ...), kind=kOutput, calls=%fused_computation.74.clone.1 | convolution fusion | flops 709558272 | bytes 1019904 | tf_op jit(solution)/shard_map/while/body/eval_jaxpr/mrj,mji->ri/dot_general | solution.py:32
  772.7 118.4 %psum.31 = f32[32]{0:T(128)S(1)} all-reduce(f32[32]{0:T(128)S(1)} %multiply_reduce_fusion), channel_id=1, replica_groups=mesh['leaf'=32,'sub'=16] {'leaf','sub'}, use_global_device_ids=true, to_apply=%region_11.12 | all-reduce | flops 32 | bytes 256 | tf_op jit(solution)/shard_map/psum | solution.py:113
  (259 shorter events, 141.6 us)
Async XLA Ops:
  0.6 262.3 %collective-permute-start = (f32[4,32,256]{2,1,0:T(8,128)}, f32[4,32,256]{2,1,0:T(8,128)S(1)}, u32[]{:S(2)}, u32[]{:S(2)}) collective-permute-start(f32[4,32,256]{2,1,0:T(8,128)} %param.7), channel_id=1, source_target_pairs={{0,41},{1,42},{2,43},{3,44},{4,45},{5,46},{6,47},{7,48},{8,49},{9,... | collective-permute-start | bytes 393224 | tf_op jit(solution)/shard_map/ppermute | solution.py:16
  8.6 260.8 %collective-permute-start.1 = (f32[4,32,256]{2,1,0:T(8,128)}, f32[4,32,256]{2,1,0:T(8,128)S(1)}, u32[]{:S(2)}, u32[]{:S(2)}) collective-permute-start(f32[4,32,256]{2,1,0:T(8,128)} %param.7), channel_id=1, source_target_pairs={{0,40},{1,41},{2,42},{3,43},{4,44},{5,45},{6,46},{7,47},{8,48},{9,... | collective-permute-start | bytes 393224 | tf_op jit(solution)/shard_map/ppermute | solution.py:16
  14.0 266.8 %collective-permute-start.2 = (f32[4,32,256]{2,1,0:T(8,128)}, f32[4,32,256]{2,1,0:T(8,128)S(1)}, u32[]{:S(2)}, u32[]{:S(2)}) collective-permute-start(f32[4,32,256]{2,1,0:T(8,128)} %param.7), channel_id=1, source_target_pairs={{0,39},{1,40},{2,41},{3,42},{4,43},{5,44},{6,45},{7,46},{8,47},{9,... | collective-permute-start | bytes 393224 | tf_op jit(solution)/shard_map/ppermute | solution.py:16
  20.2 262.6 %collective-permute-start.3 = (f32[4,32,256]{2,1,0:T(8,128)}, f32[4,32,256]{2,1,0:T(8,128)S(1)}, u32[]{:S(2)}, u32[]{:S(2)}) collective-permute-start(f32[4,32,256]{2,1,0:T(8,128)} %param.7), channel_id=1, source_target_pairs={{0,33},{1,34},{2,35},{3,36},{4,37},{5,38},{6,39},{7,40},{8,41},{9,... | collective-permute-start | bytes 393224 | tf_op jit(solution)/shard_map/ppermute | solution.py:16
  46.9 9.3 %collective-permute-start.29 = (f32[4,3,256]{2,0,1:T(4,128)}, f32[4,3,256]{2,0,1:T(4,128)S(1)}, u32[]{:S(2)}, u32[]{:S(2)}) collective-permute-start(f32[4,3,256]{2,0,1:T(4,128)} %param.8), channel_id=1, source_target_pairs={{0,33},{1,34},{2,35},{3,36},{4,37},{5,38},{6,39},{7,40},{8,41},{9,... | collective-permute-start | bytes 36872 | tf_op jit(solution)/shard_map/ppermute | solution.py:16
  71.4 8.3 collective-permute-start.32
  79.7 12.5 %collective-permute-start.33 = (f32[4,3,256]{2,0,1:T(4,128)}, f32[4,3,256]{2,0,1:T(4,128)S(1)}, u32[]{:S(2)}, u32[]{:S(2)}) collective-permute-start(f32[4,3,256]{2,0,1:T(4,128)} %param.8), channel_id=1, source_target_pairs={{0,24},{1,25},{2,26},{3,27},{4,28},{5,29},{6,30},{7,31},{8,32},{9,... | collective-permute-start | bytes 36872 | tf_op jit(solution)/shard_map/ppermute | solution.py:16
  112.2 8.2 collective-permute-start.37
  120.4 8.5 collective-permute-start.38
  140.6 11.8 %collective-permute-start.41 = (f32[4,3,256]{2,0,1:T(4,128)}, f32[4,3,256]{2,0,1:T(4,128)S(1)}, u32[]{:S(2)}, u32[]{:S(2)}) collective-permute-start(f32[4,3,256]{2,0,1:T(4,128)} %param.8), channel_id=1, source_target_pairs={{8,0},{9,1},{10,2},{11,3},{12,4},{13,5},{14,6},{15,7},{16,8},{17,9... | collective-permute-start | bytes 36872 | tf_op jit(solution)/shard_map/ppermute | solution.py:16
  160.5 8.9 collective-permute-start.43
  169.4 11.0 %collective-permute-start.44 = (f32[4,3,256]{2,0,1:T(4,128)}, f32[4,3,256]{2,0,1:T(4,128)S(1)}, u32[]{:S(2)}, u32[]{:S(2)}) collective-permute-start(f32[4,3,256]{2,0,1:T(4,128)} %param.8), channel_id=1, source_target_pairs={{24,0},{25,1},{26,2},{27,3},{28,4},{29,5},{30,6},{31,7},{32,8},{33... | collective-permute-start | bytes 36872 | tf_op jit(solution)/shard_map/ppermute | solution.py:16
  180.4 8.5 collective-permute-start.45
  188.9 19.9 %collective-permute-start.46 = (f32[4,3,256]{2,0,1:T(4,128)}, f32[4,3,256]{2,0,1:T(4,128)S(1)}, u32[]{:S(2)}, u32[]{:S(2)}) collective-permute-start(f32[4,3,256]{2,0,1:T(4,128)} %param.8), channel_id=1, source_target_pairs={{31,0},{32,1},{33,2},{34,3},{35,4},{36,5},{37,6},{38,7},{39,8},{40... | collective-permute-start | bytes 36872 | tf_op jit(solution)/shard_map/ppermute | solution.py:16
  208.8 12.0 %collective-permute-start.47 = (f32[4,3,256]{2,0,1:T(4,128)}, f32[4,3,256]{2,0,1:T(4,128)S(1)}, u32[]{:S(2)}, u32[]{:S(2)}) collective-permute-start(f32[4,3,256]{2,0,1:T(4,128)} %param.8), channel_id=1, source_target_pairs={{32,0},{33,1},{34,2},{35,3},{36,4},{37,5},{38,6},{39,7},{40,8},{41... | collective-permute-start | bytes 36872 | tf_op jit(solution)/shard_map/ppermute | solution.py:16
  226.4 9.1 %collective-permute-start.49 = (f32[4,3,256]{2,0,1:T(4,128)}, f32[4,3,256]{2,0,1:T(4,128)S(1)}, u32[]{:S(2)}, u32[]{:S(2)}) collective-permute-start(f32[4,3,256]{2,0,1:T(4,128)} %param.8), channel_id=1, source_target_pairs={{39,0},{40,1},{41,2},{42,3},{43,4},{44,5},{45,6},{46,7},{47,8},{48... | collective-permute-start | bytes 36872 | tf_op jit(solution)/shard_map/ppermute | solution.py:16
  235.5 13.2 %collective-permute-start.50 = (f32[4,3,256]{2,0,1:T(4,128)}, f32[4,3,256]{2,0,1:T(4,128)S(1)}, u32[]{:S(2)}, u32[]{:S(2)}) collective-permute-start(f32[4,3,256]{2,0,1:T(4,128)} %param.8), channel_id=1, source_target_pairs={{40,0},{41,1},{42,2},{43,3},{44,4},{45,5},{46,6},{47,7},{48,8},{49... | collective-permute-start | bytes 36872 | tf_op jit(solution)/shard_map/ppermute | solution.py:16
  248.7 8.4 collective-permute-start.51
  257.0 33.0 %collective-permute-start.4 = (f32[4,32,256]{2,1,0:T(8,128)}, f32[4,32,256]{2,1,0:T(8,128)S(1)}, u32[]{:S(2)}, u32[]{:S(2)}) collective-permute-start(f32[4,32,256]{2,1,0:T(8,128)} %param.7), channel_id=1, source_target_pairs={{0,32},{1,33},{2,34},{3,35},{4,36},{5,37},{6,38},{7,39},{8,40},{9,... | collective-permute-start | bytes 393224 | tf_op jit(solution)/shard_map/ppermute | solution.py:16
  263.0 29.1 %collective-permute-start.5 = (f32[4,32,256]{2,1,0:T(8,128)}, f32[4,32,256]{2,1,0:T(8,128)S(1)}, u32[]{:S(2)}, u32[]{:S(2)}) collective-permute-start(f32[4,32,256]{2,1,0:T(8,128)} %param.7), channel_id=1, source_target_pairs={{0,31},{1,32},{2,33},{3,34},{4,35},{5,36},{6,37},{7,38},{8,39},{9,... | collective-permute-start | bytes 393224 | tf_op jit(solution)/shard_map/ppermute | solution.py:16
  269.4 28.2 %collective-permute-start.6 = (f32[4,32,256]{2,1,0:T(8,128)S(1)}, f32[4,32,256]{2,1,0:T(8,128)S(1)}, u32[]{:S(2)}, u32[]{:S(2)}) collective-permute-start(f32[4,32,256]{2,1,0:T(8,128)S(1)} %copy-done.2), channel_id=1, source_target_pairs={{0,25},{1,26},{2,27},{3,28},{4,29},{5,30},{6,31},{7,32},{8,33},{9,... | collective-permute-start | bytes 393224 | tf_op jit(solution)/shard_map/ppermute | solution.py:16
  280.8 18.7 %collective-permute-start.7 = (f32[4,32,256]{2,1,0:T(8,128)S(1)}, f32[4,32,256]{2,1,0:T(8,128)S(1)}, u32[]{:S(2)}, u32[]{:S(2)}) collective-permute-start(f32[4,32,256]{2,1,0:T(8,128)S(1)} %copy-done.2), channel_id=1, source_target_pairs={{0,24},{1,25},{2,26},{3,27},{4,28},{5,29},{6,30},{7,31},{8,32},{9,... | collective-permute-start | bytes 393224 | tf_op jit(solution)/shard_map/ppermute | solution.py:16
  282.8 19.8 %collective-permute-start.8 = (f32[4,32,256]{2,1,0:T(8,128)S(1)}, f32[4,32,256]{2,1,0:T(8,128)S(1)}, u32[]{:S(2)}, u32[]{:S(2)}) collective-permute-start(f32[4,32,256]{2,1,0:T(8,128)S(1)} %copy-done.2), channel_id=1, source_target_pairs={{0,23},{1,24},{2,25},{3,26},{4,27},{5,28},{6,29},{7,30},{8,31},{9,... | collective-permute-start | bytes 393224 | tf_op jit(solution)/shard_map/ppermute | solution.py:16
  290.1 18.4 %collective-permute-start.9 = (f32[4,32,256]{2,1,0:T(8,128)S(1)}, f32[4,32,256]{2,1,0:T(8,128)S(1)}, u32[]{:S(2)}, u32[]{:S(2)}) collective-permute-start(f32[4,32,256]{2,1,0:T(8,128)S(1)} %copy-done.2), channel_id=1, source_target_pairs={{0,9},{1,10},{2,11},{3,12},{4,13},{5,14},{6,15},{7,16},{8,17},{9,1... | collective-permute-start | bytes 393224 | tf_op jit(solution)/shard_map/ppermute | solution.py:16
  292.1 19.5 %collective-permute-start.10 = (f32[4,32,256]{2,1,0:T(8,128)S(1)}, f32[4,32,256]{2,1,0:T(8,128)S(1)}, u32[]{:S(2)}, u32[]{:S(2)}) collective-permute-start(f32[4,32,256]{2,1,0:T(8,128)S(1)} %copy-done.2), channel_id=1, source_target_pairs={{0,8},{1,9},{2,10},{3,11},{4,12},{5,13},{6,14},{7,15},{8,16},{9,17... | collective-permute-start | bytes 393224 | tf_op jit(solution)/shard_map/ppermute | solution.py:16
  297.6 18.0 %collective-permute-start.11 = (f32[4,32,256]{2,1,0:T(8,128)S(1)}, f32[4,32,256]{2,1,0:T(8,128)S(1)}, u32[]{:S(2)}, u32[]{:S(2)}) collective-permute-start(f32[4,32,256]{2,1,0:T(8,128)S(1)} %copy-done.2), channel_id=1, source_target_pairs={{0,7},{1,8},{2,9},{3,10},{4,11},{5,12},{6,13},{7,14},{8,15},{9,16}... | collective-permute-start | bytes 393224 | tf_op jit(solution)/shard_map/ppermute | solution.py:16
  299.5 18.0 %collective-permute-start.12 = (f32[4,32,256]{2,1,0:T(8,128)S(1)}, f32[4,32,256]{2,1,0:T(8,128)S(1)}, u32[]{:S(2)}, u32[]{:S(2)}) collective-permute-start(f32[4,32,256]{2,1,0:T(8,128)S(1)} %copy-done.2), channel_id=1, source_target_pairs={{0,1},{1,2},{2,3},{3,4},{4,5},{5,6},{6,7},{7,8},{8,9},{9,10},{10,1... | collective-permute-start | bytes 393224 | tf_op jit(solution)/shard_map/ppermute | solution.py:16
  302.7 16.2 %collective-permute-start.13 = (f32[4,32,256]{2,1,0:T(8,128)S(1)}, f32[4,32,256]{2,1,0:T(8,128)S(1)}, u32[]{:S(2)}, u32[]{:S(2)}) collective-permute-start(f32[4,32,256]{2,1,0:T(8,128)S(1)} %copy-done.2), channel_id=1, source_target_pairs={{1,0},{2,1},{3,2},{4,3},{5,4},{6,5},{7,6},{8,7},{9,8},{10,9},{11,1... | collective-permute-start | bytes 393224 | tf_op jit(solution)/shard_map/ppermute | solution.py:16
  308.5 11.7 %collective-permute-start.14 = (f32[4,32,256]{2,1,0:T(8,128)S(1)}, f32[4,32,256]{2,1,0:T(8,128)S(1)}, u32[]{:S(2)}, u32[]{:S(2)}) collective-permute-start(f32[4,32,256]{2,1,0:T(8,128)S(1)} %copy-done.2), channel_id=1, source_target_pairs={{7,0},{8,1},{9,2},{10,3},{11,4},{12,5},{13,6},{14,7},{15,8},{16,9}... | collective-permute-start | bytes 393224 | tf_op jit(solution)/shard_map/ppermute | solution.py:16
  311.5 10.0 %collective-permute-start.15 = (f32[4,32,256]{2,1,0:T(8,128)S(1)}, f32[4,32,256]{2,1,0:T(8,128)S(1)}, u32[]{:S(2)}, u32[]{:S(2)}) collective-permute-start(f32[4,32,256]{2,1,0:T(8,128)S(1)} %copy-done.2), channel_id=1, source_target_pairs={{8,0},{9,1},{10,2},{11,3},{12,4},{13,5},{14,6},{15,7},{16,8},{17,9... | collective-permute-start | bytes 393224 | tf_op jit(solution)/shard_map/ppermute | solution.py:16
  317.6 9.4 %collective-permute-start.17 = (f32[4,32,256]{2,1,0:T(8,128)S(1)}, f32[4,32,256]{2,1,0:T(8,128)S(1)}, u32[]{:S(2)}, u32[]{:S(2)}) collective-permute-start(f32[4,32,256]{2,1,0:T(8,128)S(1)} %copy-done.2), channel_id=1, source_target_pairs={{23,0},{24,1},{25,2},{26,3},{27,4},{28,5},{29,6},{30,7},{31,8},{32... | collective-permute-start | bytes 393224 | tf_op jit(solution)/shard_map/ppermute | solution.py:16
  318.9 11.8 %collective-permute-start.18 = (f32[4,32,256]{2,1,0:T(8,128)S(1)}, f32[4,32,256]{2,1,0:T(8,128)S(1)}, u32[]{:S(2)}, u32[]{:S(2)}) collective-permute-start(f32[4,32,256]{2,1,0:T(8,128)S(1)} %copy-done.2), channel_id=1, source_target_pairs={{24,0},{25,1},{26,2},{27,3},{28,4},{29,5},{30,6},{31,7},{32,8},{33... | collective-permute-start | bytes 393224 | tf_op jit(solution)/shard_map/ppermute | solution.py:16
  320.2 11.7 %collective-permute-start.19 = (f32[4,32,256]{2,1,0:T(8,128)S(1)}, f32[4,32,256]{2,1,0:T(8,128)S(1)}, u32[]{:S(2)}, u32[]{:S(2)}) collective-permute-start(f32[4,32,256]{2,1,0:T(8,128)S(1)} %copy-done.2), channel_id=1, source_target_pairs={{25,0},{26,1},{27,2},{28,3},{29,4},{30,5},{31,6},{32,7},{33,8},{34... | collective-permute-start | bytes 393224 | tf_op jit(solution)/shard_map/ppermute | solution.py:16
  321.6 14.4 %collective-permute-start.20 = (f32[4,32,256]{2,1,0:T(8,128)S(1)}, f32[4,32,256]{2,1,0:T(8,128)S(1)}, u32[]{:S(2)}, u32[]{:S(2)}) collective-permute-start(f32[4,32,256]{2,1,0:T(8,128)S(1)} %copy-done.2), channel_id=1, source_target_pairs={{31,0},{32,1},{33,2},{34,3},{35,4},{36,5},{37,6},{38,7},{39,8},{40... | collective-permute-start | bytes 393224 | tf_op jit(solution)/shard_map/ppermute | solution.py:16
  323.7 19.1 %collective-permute-start.21 = (f32[4,32,256]{2,1,0:T(8,128)S(1)}, f32[4,32,256]{2,1,0:T(8,128)S(1)}, u32[]{:S(2)}, u32[]{:S(2)}) collective-permute-start(f32[4,32,256]{2,1,0:T(8,128)S(1)} %copy-done.2), channel_id=1, source_target_pairs={{32,0},{33,1},{34,2},{35,3},{36,4},{37,5},{38,6},{39,7},{40,8},{41... | collective-permute-start | bytes 393224 | tf_op jit(solution)/shard_map/ppermute | solution.py:16
  327.0 15.9 %collective-permute-start.22 = (f32[4,32,256]{2,1,0:T(8,128)S(1)}, f32[4,32,256]{2,1,0:T(8,128)S(1)}, u32[]{:S(2)}, u32[]{:S(2)}) collective-permute-start(f32[4,32,256]{2,1,0:T(8,128)S(1)} %copy-done.2), channel_id=1, source_target_pairs={{33,0},{34,1},{35,2},{36,3},{37,4},{38,5},{39,6},{40,7},{41,8},{42... | collective-permute-start | bytes 393224 | tf_op jit(solution)/shard_map/ppermute | solution.py:16
  330.7 12.8 %collective-permute-start.23 = (f32[4,32,256]{2,1,0:T(8,128)S(1)}, f32[4,32,256]{2,1,0:T(8,128)S(1)}, u32[]{:S(2)}, u32[]{:S(2)}) collective-permute-start(f32[4,32,256]{2,1,0:T(8,128)S(1)} %copy-done.2), channel_id=1, source_target_pairs={{39,0},{40,1},{41,2},{42,3},{43,4},{44,5},{45,6},{46,7},{47,8},{48... | collective-permute-start | bytes 393224 | tf_op jit(solution)/shard_map/ppermute | solution.py:16
  332.0 15.7 %collective-permute-start.24 = (f32[4,32,256]{2,1,0:T(8,128)S(1)}, f32[4,32,256]{2,1,0:T(8,128)S(1)}, u32[]{:S(2)}, u32[]{:S(2)}) collective-permute-start(f32[4,32,256]{2,1,0:T(8,128)S(1)} %copy-done.2), channel_id=1, source_target_pairs={{40,0},{41,1},{42,2},{43,3},{44,4},{45,5},{46,6},{47,7},{48,8},{49... | collective-permute-start | bytes 393224 | tf_op jit(solution)/shard_map/ppermute | solution.py:16
  335.9 11.8 %collective-permute-start.25 = (f32[4,32,256]{2,1,0:T(8,128)S(1)}, f32[4,32,256]{2,1,0:T(8,128)S(1)}, u32[]{:S(2)}, u32[]{:S(2)}) collective-permute-start(f32[4,32,256]{2,1,0:T(8,128)S(1)} %copy-done.2), channel_id=1, source_target_pairs={{41,0},{42,1},{43,2},{44,3},{45,4},{46,5},{47,6},{48,7},{49,8},{50... | collective-permute-start | bytes 393224 | tf_op jit(solution)/shard_map/ppermute | solution.py:16
  620.6 19.9 %collective-permute-start.52 = (f32[4,32,256]{2,1,0:T(8,128)S(1)}, f32[4,32,256]{2,1,0:T(8,128)S(1)}, u32[]{:S(2)}, u32[]{:S(2)}) collective-permute-start(f32[4,32,256]{2,1,0:T(8,128)S(1)} %multiply_add_fusion.2), channel_id=1, source_target_pairs={{0,41},{1,42},{2,43},{3,44},{4,45},{5,46},{6,47},{7,48},{8,49},{9,... | collective-permute-start | bytes 393224 | tf_op jit(solution)/shard_map/ppermute | solution.py:16
  625.6 21.9 %collective-permute-start.53 = (f32[4,32,256]{2,1,0:T(8,128)S(1)}, f32[4,32,256]{2,1,0:T(8,128)S(1)}, u32[]{:S(2)}, u32[]{:S(2)}) collective-permute-start(f32[4,32,256]{2,1,0:T(8,128)S(1)} %multiply_add_fusion.2), channel_id=1, source_target_pairs={{0,40},{1,41},{2,42},{3,43},{4,44},{5,45},{6,46},{7,47},{8,48},{9,... | collective-permute-start | bytes 393224 | tf_op jit(solution)/shard_map/ppermute | solution.py:16
  629.2 21.2 %collective-permute-start.54 = (f32[4,32,256]{2,1,0:T(8,128)S(1)}, f32[4,32,256]{2,1,0:T(8,128)S(1)}, u32[]{:S(2)}, u32[]{:S(2)}) collective-permute-start(f32[4,32,256]{2,1,0:T(8,128)S(1)} %multiply_add_fusion.2), channel_id=1, source_target_pairs={{0,39},{1,40},{2,41},{3,42},{4,43},{5,44},{6,45},{7,46},{8,47},{9,... | collective-permute-start | bytes 393224 | tf_op jit(solution)/shard_map/ppermute | solution.py:16
  632.6 22.1 %collective-permute-start.55 = (f32[4,32,256]{2,1,0:T(8,128)S(1)}, f32[4,32,256]{2,1,0:T(8,128)S(1)}, u32[]{:S(2)}, u32[]{:S(2)}) collective-permute-start(f32[4,32,256]{2,1,0:T(8,128)S(1)} %multiply_add_fusion.2), channel_id=1, source_target_pairs={{0,33},{1,34},{2,35},{3,36},{4,37},{5,38},{6,39},{7,40},{8,41},{9,... | collective-permute-start | bytes 393224 | tf_op jit(solution)/shard_map/ppermute | solution.py:16
  637.9 22.1 %collective-permute-start.56 = (f32[4,32,256]{2,1,0:T(8,128)S(1)}, f32[4,32,256]{2,1,0:T(8,128)S(1)}, u32[]{:S(2)}, u32[]{:S(2)}) collective-permute-start(f32[4,32,256]{2,1,0:T(8,128)S(1)} %multiply_add_fusion.2), channel_id=1, source_target_pairs={{0,32},{1,33},{2,34},{3,35},{4,36},{5,37},{6,38},{7,39},{8,40},{9,... | collective-permute-start | bytes 393224 | tf_op jit(solution)/shard_map/ppermute | solution.py:16
  640.4 23.7 %collective-permute-start.57 = (f32[4,32,256]{2,1,0:T(8,128)S(1)}, f32[4,32,256]{2,1,0:T(8,128)S(1)}, u32[]{:S(2)}, u32[]{:S(2)}) collective-permute-start(f32[4,32,256]{2,1,0:T(8,128)S(1)} %multiply_add_fusion.2), channel_id=1, source_target_pairs={{0,31},{1,32},{2,33},{3,34},{4,35},{5,36},{6,37},{7,38},{8,39},{9,... | collective-permute-start | bytes 393224 | tf_op jit(solution)/shard_map/ppermute | solution.py:16
  647.6 19.8 %collective-permute-start.58 = (f32[4,32,256]{2,1,0:T(8,128)S(1)}, f32[4,32,256]{2,1,0:T(8,128)S(1)}, u32[]{:S(2)}, u32[]{:S(2)}) collective-permute-start(f32[4,32,256]{2,1,0:T(8,128)S(1)} %multiply_add_fusion.2), channel_id=1, source_target_pairs={{0,25},{1,26},{2,27},{3,28},{4,29},{5,30},{6,31},{7,32},{8,33},{9,... | collective-permute-start | bytes 393224 | tf_op jit(solution)/shard_map/ppermute | solution.py:16
  650.4 21.0 %collective-permute-start.59 = (f32[4,32,256]{2,1,0:T(8,128)S(1)}, f32[4,32,256]{2,1,0:T(8,128)S(1)}, u32[]{:S(2)}, u32[]{:S(2)}) collective-permute-start(f32[4,32,256]{2,1,0:T(8,128)S(1)} %multiply_add_fusion.2), channel_id=1, source_target_pairs={{0,24},{1,25},{2,26},{3,27},{4,28},{5,29},{6,30},{7,31},{8,32},{9,... | collective-permute-start | bytes 393224 | tf_op jit(solution)/shard_map/ppermute | solution.py:16
  654.7 18.6 %collective-permute-start.60 = (f32[4,32,256]{2,1,0:T(8,128)S(1)}, f32[4,32,256]{2,1,0:T(8,128)S(1)}, u32[]{:S(2)}, u32[]{:S(2)}) collective-permute-start(f32[4,32,256]{2,1,0:T(8,128)S(1)} %multiply_add_fusion.2), channel_id=1, source_target_pairs={{0,23},{1,24},{2,25},{3,26},{4,27},{5,28},{6,29},{7,30},{8,31},{9,... | collective-permute-start | bytes 393224 | tf_op jit(solution)/shard_map/ppermute | solution.py:16
  659.9 20.4 %collective-permute-start.61 = (f32[4,32,256]{2,1,0:T(8,128)S(1)}, f32[4,32,256]{2,1,0:T(8,128)S(1)}, u32[]{:S(2)}, u32[]{:S(2)}) collective-permute-start(f32[4,32,256]{2,1,0:T(8,128)S(1)} %multiply_add_fusion.2), channel_id=1, source_target_pairs={{0,9},{1,10},{2,11},{3,12},{4,13},{5,14},{6,15},{7,16},{8,17},{9,1... | collective-permute-start | bytes 393224 | tf_op jit(solution)/shard_map/ppermute | solution.py:16
  664.2 18.1 %collective-permute-start.62 = (f32[4,32,256]{2,1,0:T(8,128)S(1)}, f32[4,32,256]{2,1,0:T(8,128)S(1)}, u32[]{:S(2)}, u32[]{:S(2)}) collective-permute-start(f32[4,32,256]{2,1,0:T(8,128)S(1)} %multiply_add_fusion.2), channel_id=1, source_target_pairs={{0,8},{1,9},{2,10},{3,11},{4,12},{5,13},{6,14},{7,15},{8,16},{9,17... | collective-permute-start | bytes 393224 | tf_op jit(solution)/shard_map/ppermute | solution.py:16
  667.3 19.5 %collective-permute-start.63 = (f32[4,32,256]{2,1,0:T(8,128)S(1)}, f32[4,32,256]{2,1,0:T(8,128)S(1)}, u32[]{:S(2)}, u32[]{:S(2)}) collective-permute-start(f32[4,32,256]{2,1,0:T(8,128)S(1)} %multiply_add_fusion.2), channel_id=1, source_target_pairs={{0,7},{1,8},{2,9},{3,10},{4,11},{5,12},{6,13},{7,14},{8,15},{9,16}... | collective-permute-start | bytes 393224 | tf_op jit(solution)/shard_map/ppermute | solution.py:16
  671.4 17.4 %collective-permute-start.64 = (f32[4,32,256]{2,1,0:T(8,128)S(1)}, f32[4,32,256]{2,1,0:T(8,128)S(1)}, u32[]{:S(2)}, u32[]{:S(2)}) collective-permute-start(f32[4,32,256]{2,1,0:T(8,128)S(1)} %multiply_add_fusion.2), channel_id=1, source_target_pairs={{0,1},{1,2},{2,3},{3,4},{4,5},{5,6},{6,7},{7,8},{8,9},{9,10},{10,1... | collective-permute-start | bytes 393224 | tf_op jit(solution)/shard_map/ppermute | solution.py:16
  673.4 16.7 %collective-permute-start.65 = (f32[4,32,256]{2,1,0:T(8,128)S(1)}, f32[4,32,256]{2,1,0:T(8,128)S(1)}, u32[]{:S(2)}, u32[]{:S(2)}) collective-permute-start(f32[4,32,256]{2,1,0:T(8,128)S(1)} %multiply_add_fusion.2), channel_id=1, source_target_pairs={{1,0},{2,1},{3,2},{4,3},{5,4},{6,5},{7,6},{8,7},{9,8},{10,9},{11,1... | collective-permute-start | bytes 393224 | tf_op jit(solution)/shard_map/ppermute | solution.py:16
  680.4 11.1 %collective-permute-start.66 = (f32[4,32,256]{2,1,0:T(8,128)S(1)}, f32[4,32,256]{2,1,0:T(8,128)S(1)}, u32[]{:S(2)}, u32[]{:S(2)}) collective-permute-start(f32[4,32,256]{2,1,0:T(8,128)S(1)} %multiply_add_fusion.2), channel_id=1, source_target_pairs={{7,0},{8,1},{9,2},{10,3},{11,4},{12,5},{13,6},{14,7},{15,8},{16,9}... | collective-permute-start | bytes 393224 | tf_op jit(solution)/shard_map/ppermute | solution.py:16
  682.3 10.4 %collective-permute-start.67 = (f32[4,32,256]{2,1,0:T(8,128)S(1)}, f32[4,32,256]{2,1,0:T(8,128)S(1)}, u32[]{:S(2)}, u32[]{:S(2)}) collective-permute-start(f32[4,32,256]{2,1,0:T(8,128)S(1)} %multiply_add_fusion.2), channel_id=1, source_target_pairs={{8,0},{9,1},{10,2},{11,3},{12,4},{13,5},{14,6},{15,7},{16,8},{17,9... | collective-permute-start | bytes 393224 | tf_op jit(solution)/shard_map/ppermute | solution.py:16
  688.8 9.4 %collective-permute-start.69 = (f32[4,32,256]{2,1,0:T(8,128)S(1)}, f32[4,32,256]{2,1,0:T(8,128)S(1)}, u32[]{:S(2)}, u32[]{:S(2)}) collective-permute-start(f32[4,32,256]{2,1,0:T(8,128)S(1)} %multiply_add_fusion.2), channel_id=1, source_target_pairs={{23,0},{24,1},{25,2},{26,3},{27,4},{28,5},{29,6},{30,7},{31,8},{32... | collective-permute-start | bytes 393224 | tf_op jit(solution)/shard_map/ppermute | solution.py:16
  690.1 11.0 %collective-permute-start.70 = (f32[4,32,256]{2,1,0:T(8,128)S(1)}, f32[4,32,256]{2,1,0:T(8,128)S(1)}, u32[]{:S(2)}, u32[]{:S(2)}) collective-permute-start(f32[4,32,256]{2,1,0:T(8,128)S(1)} %multiply_add_fusion.2), channel_id=1, source_target_pairs={{24,0},{25,1},{26,2},{27,3},{28,4},{29,5},{30,6},{31,7},{32,8},{33... | collective-permute-start | bytes 393224 | tf_op jit(solution)/shard_map/ppermute | solution.py:16
  691.5 12.0 %collective-permute-start.71 = (f32[4,32,256]{2,1,0:T(8,128)S(1)}, f32[4,32,256]{2,1,0:T(8,128)S(1)}, u32[]{:S(2)}, u32[]{:S(2)}) collective-permute-start(f32[4,32,256]{2,1,0:T(8,128)S(1)} %multiply_add_fusion.2), channel_id=1, source_target_pairs={{25,0},{26,1},{27,2},{28,3},{29,4},{30,5},{31,6},{32,7},{33,8},{34... | collective-permute-start | bytes 393224 | tf_op jit(solution)/shard_map/ppermute | solution.py:16
  692.8 15.0 %collective-permute-start.72 = (f32[4,32,256]{2,1,0:T(8,128)S(1)}, f32[4,32,256]{2,1,0:T(8,128)S(1)}, u32[]{:S(2)}, u32[]{:S(2)}) collective-permute-start(f32[4,32,256]{2,1,0:T(8,128)S(1)} %multiply_add_fusion.2), channel_id=1, source_target_pairs={{31,0},{32,1},{33,2},{34,3},{35,4},{36,5},{37,6},{38,7},{39,8},{40... | collective-permute-start | bytes 393224 | tf_op jit(solution)/shard_map/ppermute | solution.py:16
  694.9 16.2 %collective-permute-start.73 = (f32[4,32,256]{2,1,0:T(8,128)S(1)}, f32[4,32,256]{2,1,0:T(8,128)S(1)}, u32[]{:S(2)}, u32[]{:S(2)}) collective-permute-start(f32[4,32,256]{2,1,0:T(8,128)S(1)} %multiply_add_fusion.2), channel_id=1, source_target_pairs={{32,0},{33,1},{34,2},{35,3},{36,4},{37,5},{38,6},{39,7},{40,8},{41... | collective-permute-start | bytes 393224 | tf_op jit(solution)/shard_map/ppermute | solution.py:16
  698.2 14.3 %collective-permute-start.74 = (f32[4,32,256]{2,1,0:T(8,128)S(1)}, f32[4,32,256]{2,1,0:T(8,128)S(1)}, u32[]{:S(2)}, u32[]{:S(2)}) collective-permute-start(f32[4,32,256]{2,1,0:T(8,128)S(1)} %multiply_add_fusion.2), channel_id=1, source_target_pairs={{33,0},{34,1},{35,2},{36,3},{37,4},{38,5},{39,6},{40,7},{41,8},{42... | collective-permute-start | bytes 393224 | tf_op jit(solution)/shard_map/ppermute | solution.py:16
  701.1 14.2 %collective-permute-start.75 = (f32[4,32,256]{2,1,0:T(8,128)S(1)}, f32[4,32,256]{2,1,0:T(8,128)S(1)}, u32[]{:S(2)}, u32[]{:S(2)}) collective-permute-start(f32[4,32,256]{2,1,0:T(8,128)S(1)} %multiply_add_fusion.2), channel_id=1, source_target_pairs={{39,0},{40,1},{41,2},{42,3},{43,4},{44,5},{45,6},{46,7},{47,8},{48... | collective-permute-start | bytes 393224 | tf_op jit(solution)/shard_map/ppermute | solution.py:16
  703.5 15.4 %collective-permute-start.76 = (f32[4,32,256]{2,1,0:T(8,128)S(1)}, f32[4,32,256]{2,1,0:T(8,128)S(1)}, u32[]{:S(2)}, u32[]{:S(2)}) collective-permute-start(f32[4,32,256]{2,1,0:T(8,128)S(1)} %multiply_add_fusion.2), channel_id=1, source_target_pairs={{40,0},{41,1},{42,2},{43,3},{44,4},{45,5},{46,6},{47,7},{48,8},{49... | collective-permute-start | bytes 393224 | tf_op jit(solution)/shard_map/ppermute | solution.py:16
  707.7 13.5 %collective-permute-start.77 = (f32[4,32,256]{2,1,0:T(8,128)S(1)}, f32[4,32,256]{2,1,0:T(8,128)S(1)}, u32[]{:S(2)}, u32[]{:S(2)}) collective-permute-start(f32[4,32,256]{2,1,0:T(8,128)S(1)} %multiply_add_fusion.2), channel_id=1, source_target_pairs={{41,0},{42,1},{43,2},{44,3},{45,4},{46,5},{47,6},{48,7},{49,8},{50... | collective-permute-start | bytes 393224 | tf_op jit(solution)/shard_map/ppermute | solution.py:16
  (28 other events, 1652.6 us)
where the time goes:
time: 895 us; the launch traced here: 892 us
  blocking collectives  339 us (38%)
  starting transfers between devices  287 us (32%)
  waiting for transfers between devices  154 us (17%)
  matrix products  79.9 us (9%)
  local copies, waits for them, and re-layouts  20.7 us (2%)
    ppermute x78, starting transfers between devices, passed_along(): return lax.ppermute(block, axis, route)  287 us
    psum x2, blocking collectives, squares(): return lax.psum(column_sums(residual, residual), ('leaf', 'sub'))  221 us
    ppermute x78, waiting for transfers between devices, passed_along(): return lax.ppermute(block, axis, route)  154 us
    psum x1, blocking collectives, per_device(): curve = lax.psum(column_sums(direction, image_vec), ('leaf', 'sub'))  118 us
    dot_general x8, matrix products, apply_box(): jnp.einsum('mrj,mji->ri', near_values, kernel, precision=lax.Precision.HI...  79.9 us
  transfers between devices with their start and end apart: 78, of which 42 were waited for; matrix products, arithmetic and copies ran while one was open for 1% of the time, Pallas kernels for 0%

commit v1 on v0

--- a/solution.py
+++ b/solution.py
@@ -110,7 +110,7 @@
         near_values = gathered[positions] * present[:, :, None, None]
         products = lax.map(apply_box, (points, others, near_values))
         image_vec = KERNEL_SCALE * products + NOISE_LEVEL * direction
-        curve = lax.psum(column_sums(direction, image_vec), ("leaf", "sub"))
+        curve = jnp.sum(lax.all_gather(column_sums(direction, image_vec), ("leaf", "sub")), axis=0)
         step_size = norm_now / curve
         solution_field = solution_field + spread(step_size) * direction
         residual = residual - spread(step_size) * image_vec

time: 895 us -> 1600 us (1.79)
  waiting for transfers between devices: 154 us -> 959 us
  blocking collectives: 339 us -> 223 us
    unnamed x0 -> x4, waiting for transfers between devices: none -> 806 us
    psum x1 -> x0, blocking collectives: 118 us -> none  [per_device(): curve = lax.psum(column_sums(direction, image_vec), ('leaf', 'sub'))]
  transfers between devices with their start and end apart: 78 -> 80, of which waited for: 42 -> 43; matrix products, arithmetic and copies ran while one was open for 1% -> 0% of each run, Pallas kernels for 0% -> 0%
where the time goes in v1:
time: 1600 us; the launch traced here: 1590 us
  waiting for transfers between devices  959 us (60%)
  starting transfers between devices  284 us (18%)
  blocking collectives  223 us (14%)
  matrix products  79.9 us (5%)
  local copies, waits for them, and re-layouts  24.5 us (2%)
    unnamed x4, waiting for transfers between devices  806 us
    ppermute x78, starting transfers between devices, passed_along(): return lax.ppermute(block, axis, route)  283 us
    psum x2, blocking collectives, squares(): return lax.psum(column_sums(residual, residual), ('leaf', 'sub'))  223 us
    ppermute x78, waiting for transfers between devices, passed_along(): return lax.ppermute(block, axis, route)  153 us
    dot_general x8, matrix products, apply_box(): jnp.einsum('mrj,mji->ri', near_values, kernel, precision=lax.Precision.HI...  79.9 us
  transfers between devices with their start and end apart: 80, of which 43 were waited for; matrix products, arithmetic and copies ran while one was open for 0% of the time, Pallas kernels for 0%

profile of v1, /device:TPU:1, one launch (start us, length us, event | category | flops | bytes accessed | tf_op | source)
XLA Modules:
  0.0 1594.9 jit_solution(5876018009787574605)
XLA Ops:
  7.2 7.8 collective-permute-start
  15.1 5.4 collective-permute-start.1
  20.5 6.2 collective-permute-start.2
  26.7 5.7 collective-permute-start.3
  32.4 4.2 collective-permute-start.26
  38.8 6.3 collective-permute-start.27
  46.1 6.2 collective-permute-start.28
  53.3 8.3 collective-permute-start.29
  62.7 7.1 collective-permute-start.30
  70.8 6.0 collective-permute-start.31
  77.9 7.3 collective-permute-start.32
  86.2 11.5 collective-permute-start.33
  98.7 4.4 collective-permute-start.34
  104.1 6.2 collective-permute-start.35
  111.4 6.2 collective-permute-start.36
  118.6 5.7 collective-permute-start.37
  126.8 4.5 collective-permute-start.38
  131.4 4.0 collective-permute-done.38
  140.0 5.0 collective-permute-start.40
  147.0 5.9 collective-permute-start.41
  153.0 5.9 collective-permute-done.41
  160.8 6.2 collective-permute-done.42
  168.3 7.6 collective-permute-done.43
  177.2 9.7 collective-permute-done.44
  188.2 7.2 collective-permute-done.45
  196.7 18.6 %collective-permute-done.46 = f32[4,3,256]{2,0,1:T(4,128)S(1)} collective-permute-done((f32[4,3,256]{2,0,1:T(4,128)}, f32[4,3,256]{2,0,1:T(4,128)S(1)}, u32[]{:S(2)}, u32[]{:S(2)}) %collective-permute-start.46) | collective-permute-done | bytes 12320 | tf_op jit(solution)/shard_map/ppermute | solution.py:16
  216.6 10.7 collective-permute-done.47
  228.6 4.2 collective-permute-done.48
  234.1 7.8 collective-permute-done.49
  243.2 11.9 collective-permute-done.50
  256.4 7.1 collective-permute-done.51
  263.5 4.1 collective-permute-start.4
  269.4 6.4 collective-permute-start.5
  275.9 11.4 collective-permute-start.6
  289.3 7.2 collective-permute-start.8
  298.5 5.5 collective-permute-start.10
  309.1 5.8 collective-permute-start.13
  318.0 4.0 collective-permute-start.15
  343.9 5.4 collective-permute-done.21
  349.9 4.2 collective-permute-done.24
  361.5 43.8 %while.24 = (s32[]{:T(128)}, f32[4,32,256]{2,1,0:T(8,128)S(1)}, f32[4,27,32,256]{3,2,1,0:T(8,128)}, f32[4,27,3,256]{3,1,2,0:T(8,128)}, f32[4,3,256]{2,0,1:T(4,128)S(1)}, /*index=5*/s32[]{:T(128)}, s32[]{:T(128)}, s32[]{}, s32[]{}) while((s32[]{:T(128)}, f32[4,32,256]{2,1,0:T(8,128)S(1)}, f32[4,27,32,256]{3,2,1,0:T(8,128)}, ...), condition=%wide.region_3.4_spmd, body=%wide.region_2.3_spmd.sunk | while | flops 709558272 | bytes 1357957 | solution.py:111
  362.5 10.0 fusion.104
  373.5 10.0 fusion.104
  384.4 10.0 fusion.104
  395.4 10.0 fusion.104
  406.5 121.2 %psum.14 = f32[32]{0:T(128)S(1)} all-reduce(f32[32]{0:T(128)S(1)} %get-tuple-element.155), channel_id=1, replica_groups=mesh['leaf'=32,'sub'=16] {'leaf','sub'}, use_global_device_ids=true, to_apply=%region_1.2 | all-reduce | flops 32 | bytes 256 | tf_op jit(solution)/shard_map/psum | solution.py:84
  527.8 343.8 %all-reduce.5.cloned.1.call-done = f32[16384]{0:T(1024)} async-done(((f32[16384]{0:T(1024)}), f32[16384]{0:T(1024)}) %all-reduce.5.cloned.1.call-update) | async-done | bytes 65552
  872.8 101.5 %psum.15 = f32[32]{0:T(128)S(1)} all-reduce(f32[32]{0:T(128)S(1)} %multiply_reduce_fusion.1), channel_id=1, replica_groups=mesh['leaf'=32,'sub'=16] {'leaf','sub'}, use_global_device_ids=true, to_apply=%region_7.8 | all-reduce | flops 32 | bytes 256 | tf_op jit(solution)/shard_map/psum | solution.py:84
  978.5 4.5 collective-permute-start.53
  983.0 4.7 collective-permute-start.54
  987.8 4.2 collective-permute-start.55
  993.5 6.6 collective-permute-start.57
  1002.5 5.2 collective-permute-start.59
  1011.1 4.2 collective-permute-start.61
  1018.5 4.4 collective-permute-start.63
  1024.9 7.0 collective-permute-start.65
  1033.9 4.4 collective-permute-start.67
  1063.2 4.4 collective-permute-done.75
  1079.2 43.9 %while.25 = (s32[]{:T(128)}, f32[4,32,256]{2,1,0:T(8,128)S(1)}, f32[4,27,32,256]{3,2,1,0:T(8,128)}, f32[4,27,3,256]{3,1,2,0:T(8,128)}, f32[4,3,256]{2,0,1:T(4,128)S(1)}, /*index=5*/s32[]{:T(128)}, s32[]{:T(128)}, s32[]{}, s32[]{}) while((s32[]{:T(128)}, f32[4,32,256]{2,1,0:T(8,128)S(1)}, f32[4,27,32,256]{3,2,1,0:T(8,128)}, ...), condition=%wide.region_9.10_spmd, body=%wide.region_8.9_spmd.sunk | while | flops 709558272 | bytes 1357957 | solution.py:111
  1080.2 10.0 fusion.107
  1091.2 10.0 fusion.107
  1102.1 10.0 fusion.107
  1113.1 10.0 fusion.107
  1124.2 462.0 %all-reduce.7.cloned.1.call-done = f32[16384]{0:T(1024)} async-done(((f32[16384]{0:T(1024)}), f32[16384]{0:T(1024)}) %all-reduce.7.cloned.1.call-update) | async-done | bytes 65552
  (276 shorter events, 145.7 us)
Async XLA Ops:
  7.2 864.4 %all-reduce.5.cloned.1.call-start = ((), (), s32[]{:S(2)}) async-start(), calls=%async_computation | async-start | bytes 131072
  7.2 262.2 %collective-permute-start = (f32[4,32,256]{2,1,0:T(8,128)}, f32[4,32,256]{2,1,0:T(8,128)S(1)}, u32[]{:S(2)}, u32[]{:S(2)}) collective-permute-start(f32[4,32,256]{2,1,0:T(8,128)} %param.7), channel_id=1, source_target_pairs={{0,41},{1,42},{2,43},{3,44},{4,45},{5,46},{6,47},{7,48},{8,49},{9,... | collective-permute-start | bytes 393224 | tf_op jit(solution)/shard_map/ppermute | solution.py:16
  15.1 260.8 %collective-permute-start.1 = (f32[4,32,256]{2,1,0:T(8,128)}, f32[4,32,256]{2,1,0:T(8,128)S(1)}, u32[]{:S(2)}, u32[]{:S(2)}) collective-permute-start(f32[4,32,256]{2,1,0:T(8,128)} %param.7), channel_id=1, source_target_pairs={{0,40},{1,41},{2,42},{3,43},{4,44},{5,45},{6,46},{7,47},{8,48},{9,... | collective-permute-start | bytes 393224 | tf_op jit(solution)/shard_map/ppermute | solution.py:16
  20.5 266.8 %collective-permute-start.2 = (f32[4,32,256]{2,1,0:T(8,128)}, f32[4,32,256]{2,1,0:T(8,128)S(1)}, u32[]{:S(2)}, u32[]{:S(2)}) collective-permute-start(f32[4,32,256]{2,1,0:T(8,128)} %param.7), channel_id=1, source_target_pairs={{0,39},{1,40},{2,41},{3,42},{4,43},{5,44},{6,45},{7,46},{8,47},{9,... | collective-permute-start | bytes 393224 | tf_op jit(solution)/shard_map/ppermute | solution.py:16
  26.7 262.6 %collective-permute-start.3 = (f32[4,32,256]{2,1,0:T(8,128)}, f32[4,32,256]{2,1,0:T(8,128)S(1)}, u32[]{:S(2)}, u32[]{:S(2)}) collective-permute-start(f32[4,32,256]{2,1,0:T(8,128)} %param.7), channel_id=1, source_target_pairs={{0,33},{1,34},{2,35},{3,36},{4,37},{5,38},{6,39},{7,40},{8,41},{9,... | collective-permute-start | bytes 393224 | tf_op jit(solution)/shard_map/ppermute | solution.py:16
  53.3 9.3 collective-permute-start.29
  86.2 12.5 collective-permute-start.33
  126.8 8.5 collective-permute-start.38
  147.0 11.8 collective-permute-start.41
  167.0 8.9 collective-permute-start.43
  175.9 11.0 collective-permute-start.44
  186.9 8.5 collective-permute-start.45
  195.4 19.9 %collective-permute-start.46 = (f32[4,3,256]{2,0,1:T(4,128)}, f32[4,3,256]{2,0,1:T(4,128)S(1)}, u32[]{:S(2)}, u32[]{:S(2)}) collective-permute-start(f32[4,3,256]{2,0,1:T(4,128)} %param.8), channel_id=1, source_target_pairs={{31,0},{32,1},{33,2},{34,3},{35,4},{36,5},{37,6},{38,7},{39,8},{40... | collective-permute-start | bytes 36872 | tf_op jit(solution)/shard_map/ppermute | solution.py:16
  215.3 12.0 collective-permute-start.47
  232.8 9.1 collective-permute-start.49
  241.9 13.2 collective-permute-start.50
  255.1 8.4 collective-permute-start.51
  263.5 33.1 %collective-permute-start.4 = (f32[4,32,256]{2,1,0:T(8,128)}, f32[4,32,256]{2,1,0:T(8,128)S(1)}, u32[]{:S(2)}, u32[]{:S(2)}) collective-permute-start(f32[4,32,256]{2,1,0:T(8,128)} %param.7), channel_id=1, source_target_pairs={{0,32},{1,33},{2,34},{3,35},{4,36},{5,37},{6,38},{7,39},{8,40},{9,... | collective-permute-start | bytes 393224 | tf_op jit(solution)/shard_map/ppermute | solution.py:16
  269.4 29.1 %collective-permute-start.5 = (f32[4,32,256]{2,1,0:T(8,128)}, f32[4,32,256]{2,1,0:T(8,128)S(1)}, u32[]{:S(2)}, u32[]{:S(2)}) collective-permute-start(f32[4,32,256]{2,1,0:T(8,128)} %param.7), channel_id=1, source_target_pairs={{0,31},{1,32},{2,33},{3,34},{4,35},{5,36},{6,37},{7,38},{8,39},{9,... | collective-permute-start | bytes 393224 | tf_op jit(solution)/shard_map/ppermute | solution.py:16
  275.9 28.2 %collective-permute-start.6 = (f32[4,32,256]{2,1,0:T(8,128)S(1)}, f32[4,32,256]{2,1,0:T(8,128)S(1)}, u32[]{:S(2)}, u32[]{:S(2)}) collective-permute-start(f32[4,32,256]{2,1,0:T(8,128)S(1)} %copy-done.2), channel_id=1, source_target_pairs={{0,25},{1,26},{2,27},{3,28},{4,29},{5,30},{6,31},{7,32},{8,33},{9,... | collective-permute-start | bytes 393224 | tf_op jit(solution)/shard_map/ppermute | solution.py:16
  287.3 18.7 %collective-permute-start.7 = (f32[4,32,256]{2,1,0:T(8,128)S(1)}, f32[4,32,256]{2,1,0:T(8,128)S(1)}, u32[]{:S(2)}, u32[]{:S(2)}) collective-permute-start(f32[4,32,256]{2,1,0:T(8,128)S(1)} %copy-done.2), channel_id=1, source_target_pairs={{0,24},{1,25},{2,26},{3,27},{4,28},{5,29},{6,30},{7,31},{8,32},{9,... | collective-permute-start | bytes 393224 | tf_op jit(solution)/shard_map/ppermute | solution.py:16
  289.3 19.8 %collective-permute-start.8 = (f32[4,32,256]{2,1,0:T(8,128)S(1)}, f32[4,32,256]{2,1,0:T(8,128)S(1)}, u32[]{:S(2)}, u32[]{:S(2)}) collective-permute-start(f32[4,32,256]{2,1,0:T(8,128)S(1)} %copy-done.2), channel_id=1, source_target_pairs={{0,23},{1,24},{2,25},{3,26},{4,27},{5,28},{6,29},{7,30},{8,31},{9,... | collective-permute-start | bytes 393224 | tf_op jit(solution)/shard_map/ppermute | solution.py:16
  296.6 18.4 %collective-permute-start.9 = (f32[4,32,256]{2,1,0:T(8,128)S(1)}, f32[4,32,256]{2,1,0:T(8,128)S(1)}, u32[]{:S(2)}, u32[]{:S(2)}) collective-permute-start(f32[4,32,256]{2,1,0:T(8,128)S(1)} %copy-done.2), channel_id=1, source_target_pairs={{0,9},{1,10},{2,11},{3,12},{4,13},{5,14},{6,15},{7,16},{8,17},{9,1... | collective-permute-start | bytes 393224 | tf_op jit(solution)/shard_map/ppermute | solution.py:16
  298.5 19.5 %collective-permute-start.10 = (f32[4,32,256]{2,1,0:T(8,128)S(1)}, f32[4,32,256]{2,1,0:T(8,128)S(1)}, u32[]{:S(2)}, u32[]{:S(2)}) collective-permute-start(f32[4,32,256]{2,1,0:T(8,128)S(1)} %copy-done.2), channel_id=1, source_target_pairs={{0,8},{1,9},{2,10},{3,11},{4,12},{5,13},{6,14},{7,15},{8,16},{9,17... | collective-permute-start | bytes 393224 | tf_op jit(solution)/shard_map/ppermute | solution.py:16
  304.0 18.0 %collective-permute-start.11 = (f32[4,32,256]{2,1,0:T(8,128)S(1)}, f32[4,32,256]{2,1,0:T(8,128)S(1)}, u32[]{:S(2)}, u32[]{:S(2)}) collective-permute-start(f32[4,32,256]{2,1,0:T(8,128)S(1)} %copy-done.2), channel_id=1, source_target_pairs={{0,7},{1,8},{2,9},{3,10},{4,11},{5,12},{6,13},{7,14},{8,15},{9,16}... | collective-permute-start | bytes 393224 | tf_op jit(solution)/shard_map/ppermute | solution.py:16
  306.0 18.0 %collective-permute-start.12 = (f32[4,32,256]{2,1,0:T(8,128)S(1)}, f32[4,32,256]{2,1,0:T(8,128)S(1)}, u32[]{:S(2)}, u32[]{:S(2)}) collective-permute-start(f32[4,32,256]{2,1,0:T(8,128)S(1)} %copy-done.2), channel_id=1, source_target_pairs={{0,1},{1,2},{2,3},{3,4},{4,5},{5,6},{6,7},{7,8},{8,9},{9,10},{10,1... | collective-permute-start | bytes 393224 | tf_op jit(solution)/shard_map/ppermute | solution.py:16
  309.1 16.2 %collective-permute-start.13 = (f32[4,32,256]{2,1,0:T(8,128)S(1)}, f32[4,32,256]{2,1,0:T(8,128)S(1)}, u32[]{:S(2)}, u32[]{:S(2)}) collective-permute-start(f32[4,32,256]{2,1,0:T(8,128)S(1)} %copy-done.2), channel_id=1, source_target_pairs={{1,0},{2,1},{3,2},{4,3},{5,4},{6,5},{7,6},{8,7},{9,8},{10,9},{11,1... | collective-permute-start | bytes 393224 | tf_op jit(solution)/shard_map/ppermute | solution.py:16
  315.0 11.7 collective-permute-start.14
  318.0 10.0 collective-permute-start.15
  324.0 9.4 collective-permute-start.17
  325.4 11.8 collective-permute-start.18
  326.7 11.7 collective-permute-start.19
  328.0 14.4 collective-permute-start.20
  330.2 19.1 %collective-permute-start.21 = (f32[4,32,256]{2,1,0:T(8,128)S(1)}, f32[4,32,256]{2,1,0:T(8,128)S(1)}, u32[]{:S(2)}, u32[]{:S(2)}) collective-permute-start(f32[4,32,256]{2,1,0:T(8,128)S(1)} %copy-done.2), channel_id=1, source_target_pairs={{32,0},{33,1},{34,2},{35,3},{36,4},{37,5},{38,6},{39,7},{40,8},{41... | collective-permute-start | bytes 393224 | tf_op jit(solution)/shard_map/ppermute | solution.py:16
  333.4 15.9 collective-permute-start.22
  337.1 12.8 collective-permute-start.23
  338.4 15.7 collective-permute-start.24
  342.4 11.8 collective-permute-start.25
  406.5 1179.7 %all-reduce.7.cloned.1.call-start = ((), (), s32[]{:S(2)}) async-start(), calls=%async_computation.1 | async-start | bytes 131072
  975.0 18.5 %collective-permute-start.52 = (f32[4,32,256]{2,1,0:T(8,128)S(1)}, f32[4,32,256]{2,1,0:T(8,128)S(1)}, u32[]{:S(2)}, u32[]{:S(2)}) collective-permute-start(f32[4,32,256]{2,1,0:T(8,128)S(1)} %multiply_add_fusion.2), channel_id=1, source_target_pairs={{0,41},{1,42},{2,43},{3,44},{4,45},{5,46},{6,47},{7,48},{8,49},{9,... | collective-permute-start | bytes 393224 | tf_op jit(solution)/shard_map/ppermute | solution.py:16
  978.5 21.7 %collective-permute-start.53 = (f32[4,32,256]{2,1,0:T(8,128)S(1)}, f32[4,32,256]{2,1,0:T(8,128)S(1)}, u32[]{:S(2)}, u32[]{:S(2)}) collective-permute-start(f32[4,32,256]{2,1,0:T(8,128)S(1)} %multiply_add_fusion.2), channel_id=1, source_target_pairs={{0,40},{1,41},{2,42},{3,43},{4,44},{5,45},{6,46},{7,47},{8,48},{9,... | collective-permute-start | bytes 393224 | tf_op jit(solution)/shard_map/ppermute | solution.py:16
  983.0 19.4 %collective-permute-start.54 = (f32[4,32,256]{2,1,0:T(8,128)S(1)}, f32[4,32,256]{2,1,0:T(8,128)S(1)}, u32[]{:S(2)}, u32[]{:S(2)}) collective-permute-start(f32[4,32,256]{2,1,0:T(8,128)S(1)} %multiply_add_fusion.2), channel_id=1, source_target_pairs={{0,39},{1,40},{2,41},{3,42},{4,43},{5,44},{6,45},{7,46},{8,47},{9,... | collective-permute-start | bytes 393224 | tf_op jit(solution)/shard_map/ppermute | solution.py:16
  987.8 20.0 %collective-permute-start.55 = (f32[4,32,256]{2,1,0:T(8,128)S(1)}, f32[4,32,256]{2,1,0:T(8,128)S(1)}, u32[]{:S(2)}, u32[]{:S(2)}) collective-permute-start(f32[4,32,256]{2,1,0:T(8,128)S(1)} %multiply_add_fusion.2), channel_id=1, source_target_pairs={{0,33},{1,34},{2,35},{3,36},{4,37},{5,38},{6,39},{7,40},{8,41},{9,... | collective-permute-start | bytes 393224 | tf_op jit(solution)/shard_map/ppermute | solution.py:16
  991.9 19.2 %collective-permute-start.56 = (f32[4,32,256]{2,1,0:T(8,128)S(1)}, f32[4,32,256]{2,1,0:T(8,128)S(1)}, u32[]{:S(2)}, u32[]{:S(2)}) collective-permute-start(f32[4,32,256]{2,1,0:T(8,128)S(1)} %multiply_add_fusion.2), channel_id=1, source_target_pairs={{0,32},{1,33},{2,34},{3,35},{4,36},{5,37},{6,38},{7,39},{8,40},{9,... | collective-permute-start | bytes 393224 | tf_op jit(solution)/shard_map/ppermute | solution.py:16
  993.5 21.9 %collective-permute-start.57 = (f32[4,32,256]{2,1,0:T(8,128)S(1)}, f32[4,32,256]{2,1,0:T(8,128)S(1)}, u32[]{:S(2)}, u32[]{:S(2)}) collective-permute-start(f32[4,32,256]{2,1,0:T(8,128)S(1)} %multiply_add_fusion.2), channel_id=1, source_target_pairs={{0,31},{1,32},{2,33},{3,34},{4,35},{5,36},{6,37},{7,38},{8,39},{9,... | collective-permute-start | bytes 393224 | tf_op jit(solution)/shard_map/ppermute | solution.py:16
  1000.2 18.3 %collective-permute-start.58 = (f32[4,32,256]{2,1,0:T(8,128)S(1)}, f32[4,32,256]{2,1,0:T(8,128)S(1)}, u32[]{:S(2)}, u32[]{:S(2)}) collective-permute-start(f32[4,32,256]{2,1,0:T(8,128)S(1)} %multiply_add_fusion.2), channel_id=1, source_target_pairs={{0,25},{1,26},{2,27},{3,28},{4,29},{5,30},{6,31},{7,32},{8,33},{9,... | collective-permute-start | bytes 393224 | tf_op jit(solution)/shard_map/ppermute | solution.py:16
  1002.5 20.5 %collective-permute-start.59 = (f32[4,32,256]{2,1,0:T(8,128)S(1)}, f32[4,32,256]{2,1,0:T(8,128)S(1)}, u32[]{:S(2)}, u32[]{:S(2)}) collective-permute-start(f32[4,32,256]{2,1,0:T(8,128)S(1)} %multiply_add_fusion.2), channel_id=1, source_target_pairs={{0,24},{1,25},{2,26},{3,27},{4,28},{5,29},{6,30},{7,31},{8,32},{9,... | collective-permute-start | bytes 393224 | tf_op jit(solution)/shard_map/ppermute | solution.py:16
  1007.7 17.2 %collective-permute-start.60 = (f32[4,32,256]{2,1,0:T(8,128)S(1)}, f32[4,32,256]{2,1,0:T(8,128)S(1)}, u32[]{:S(2)}, u32[]{:S(2)}) collective-permute-start(f32[4,32,256]{2,1,0:T(8,128)S(1)} %multiply_add_fusion.2), channel_id=1, source_target_pairs={{0,23},{1,24},{2,25},{3,26},{4,27},{5,28},{6,29},{7,30},{8,31},{9,... | collective-permute-start | bytes 393224 | tf_op jit(solution)/shard_map/ppermute | solution.py:16
  1011.1 20.8 %collective-permute-start.61 = (f32[4,32,256]{2,1,0:T(8,128)S(1)}, f32[4,32,256]{2,1,0:T(8,128)S(1)}, u32[]{:S(2)}, u32[]{:S(2)}) collective-permute-start(f32[4,32,256]{2,1,0:T(8,128)S(1)} %multiply_add_fusion.2), channel_id=1, source_target_pairs={{0,9},{1,10},{2,11},{3,12},{4,13},{5,14},{6,15},{7,16},{8,17},{9,1... | collective-permute-start | bytes 393224 | tf_op jit(solution)/shard_map/ppermute | solution.py:16
  1015.4 18.5 %collective-permute-start.62 = (f32[4,32,256]{2,1,0:T(8,128)S(1)}, f32[4,32,256]{2,1,0:T(8,128)S(1)}, u32[]{:S(2)}, u32[]{:S(2)}) collective-permute-start(f32[4,32,256]{2,1,0:T(8,128)S(1)} %multiply_add_fusion.2), channel_id=1, source_target_pairs={{0,8},{1,9},{2,10},{3,11},{4,12},{5,13},{6,14},{7,15},{8,16},{9,17... | collective-permute-start | bytes 393224 | tf_op jit(solution)/shard_map/ppermute | solution.py:16
  1018.5 19.8 %collective-permute-start.63 = (f32[4,32,256]{2,1,0:T(8,128)S(1)}, f32[4,32,256]{2,1,0:T(8,128)S(1)}, u32[]{:S(2)}, u32[]{:S(2)}) collective-permute-start(f32[4,32,256]{2,1,0:T(8,128)S(1)} %multiply_add_fusion.2), channel_id=1, source_target_pairs={{0,7},{1,8},{2,9},{3,10},{4,11},{5,12},{6,13},{7,14},{8,15},{9,16}... | collective-permute-start | bytes 393224 | tf_op jit(solution)/shard_map/ppermute | solution.py:16
  1023.0 17.4 %collective-permute-start.64 = (f32[4,32,256]{2,1,0:T(8,128)S(1)}, f32[4,32,256]{2,1,0:T(8,128)S(1)}, u32[]{:S(2)}, u32[]{:S(2)}) collective-permute-start(f32[4,32,256]{2,1,0:T(8,128)S(1)} %multiply_add_fusion.2), channel_id=1, source_target_pairs={{0,1},{1,2},{2,3},{3,4},{4,5},{5,6},{6,7},{7,8},{8,9},{9,10},{10,1... | collective-permute-start | bytes 393224 | tf_op jit(solution)/shard_map/ppermute | solution.py:16
  1024.9 16.7 %collective-permute-start.65 = (f32[4,32,256]{2,1,0:T(8,128)S(1)}, f32[4,32,256]{2,1,0:T(8,128)S(1)}, u32[]{:S(2)}, u32[]{:S(2)}) collective-permute-start(f32[4,32,256]{2,1,0:T(8,128)S(1)} %multiply_add_fusion.2), channel_id=1, source_target_pairs={{1,0},{2,1},{3,2},{4,3},{5,4},{6,5},{7,6},{8,7},{9,8},{10,9},{11,1... | collective-permute-start | bytes 393224 | tf_op jit(solution)/shard_map/ppermute | solution.py:16
  1031.9 11.1 collective-permute-start.66
  1033.9 10.4 collective-permute-start.67
  1040.3 9.4 collective-permute-start.69
  1041.7 11.0 collective-permute-start.70
  1043.0 11.0 collective-permute-start.71
  1044.3 13.9 collective-permute-start.72
  1046.5 16.3 %collective-permute-start.73 = (f32[4,32,256]{2,1,0:T(8,128)S(1)}, f32[4,32,256]{2,1,0:T(8,128)S(1)}, u32[]{:S(2)}, u32[]{:S(2)}) collective-permute-start(f32[4,32,256]{2,1,0:T(8,128)S(1)} %multiply_add_fusion.2), channel_id=1, source_target_pairs={{32,0},{33,1},{34,2},{35,3},{36,4},{37,5},{38,6},{39,7},{40,8},{41... | collective-permute-start | bytes 393224 | tf_op jit(solution)/shard_map/ppermute | solution.py:16
  1049.7 13.4 collective-permute-start.74
  1052.7 14.8 collective-permute-start.75
  1054.0 16.7 %collective-permute-start.76 = (f32[4,32,256]{2,1,0:T(8,128)S(1)}, f32[4,32,256]{2,1,0:T(8,128)S(1)}, u32[]{:S(2)}, u32[]{:S(2)}) collective-permute-start(f32[4,32,256]{2,1,0:T(8,128)S(1)} %multiply_add_fusion.2), channel_id=1, source_target_pairs={{40,0},{41,1},{42,2},{43,3},{44,4},{45,5},{46,6},{47,7},{48,8},{49... | collective-permute-start | bytes 393224 | tf_op jit(solution)/shard_map/ppermute | solution.py:16
  1058.2 13.6 collective-permute-start.77
  (32 other events, 3385.5 us)
Sparse Core Ops, SparseCore 0:
  406.6 464.9 all-reduce.4
  1124.3 461.8 all-reduce.6
